TPU v7x, 256 devices: a whole 4x4x8 slice. The times are simulated.
256 devices in a mesh: dp: 32 (over z_lo, y, x), tensor: 8 (over z_hi, core).
Axes of the slice: x: 4, y: 4, z: 8 (z_hi: 4, z_lo: 2; z = z_hi * 2 + z_lo), core: 2. Of those that a mesh axis runs over, the one named last changes fastest.
Arguments:
- embeds: bfloat16 [512, 4608], P('dp'), may hold values from -6 to 6
- owner: int32 [64, 8], P('dp'), may hold values from 0 to 7, each once within a row
- pairs: int32 [64, 56, 2], P('dp'), may hold values from 0 to 7, as said below
- pref_weight: bfloat16 [2, 4608, 4608], P(None, 'dp', 'tensor'), may hold values from -0.0625 to 0.0625
- pref_bias: float32 [4608], P('tensor'), may hold values from -3 to 3
- pref_out: float32 [4608], P('tensor'), may hold values from -0.375 to 0.375
- logratio: float32 [512], P('dp'), may hold values from -3 to 3
- attn_out: bfloat16 [32768, 4096], P('dp', 'tensor'), may hold values from -6 to 6
- grad_out: bfloat16 [32768, 4608], P('dp', 'tensor'), may hold values from -6 to 6
- w_out: bfloat16 [4608, 4096], P('dp', 'tensor'), may hold values from -0.09375 to 0.09375
Outputs:
- d_attn: bfloat16 [32768, 4096], P('dp', 'tensor')
- o_grad: float32 [4608, 4096], P('dp', 'tensor')
Inputs may be any that keep to these rules, and one draw needn't show every extreme that they name: `pairs`: the two numbers of a pair differ. Each row of owner names every number once.
All inputs are finite; a program needn't handle non-finite values.
Results may differ from a plain program's by a relative error of at most 0.0049.
Values may be sent and summed in bfloat16 or wider, within the bound.
No kernel may reach another device: no remote copies, remote signals or barrier semaphores. Data moves between devices by JAX's collectives and lax.ppermute only.
A program may use at most 128 MiB of HBM per device.

v0:
```python
import jax
import jax.numpy as jnp
from jax import lax
from jax.sharding import PartitionSpec as P

eta_scale = 2.0


def shards(
    embeds, owner, pairs, pref_weight, pref_bias, pref_out, logratio, attn_out, grad_out, w_out
):
    resp_dev = embeds.shape[0]
    prompts_dev = owner.shape[0]
    groups = owner.shape[1]
    npairs = pairs.shape[1]
    width_local = pref_weight.shape[2]
    features = lax.all_gather(grad_out, "tensor", axis=1, tiled=True)
    base = (jnp.arange(prompts_dev, dtype=jnp.int32) * groups)[:, None]
    row_a = base + jnp.take_along_axis(owner, pairs[:, :, 0], axis=1)
    row_b = base + jnp.take_along_axis(owner, pairs[:, :, 1], axis=1)
    left = embeds[row_a.reshape(-1)]
    right = embeds[row_b.reshape(-1)]
    piece = lax.all_gather(pref_weight, "dp", axis=1, tiled=True)
    upper = jnp.dot(left, piece[0], preferred_element_type=jnp.float32)
    lower = jnp.dot(right, piece[1], preferred_element_type=jnp.float32)
    pre = (upper + lower).reshape(prompts_dev, npairs, width_local)
    hidden = jax.nn.gelu(pre + pref_bias)
    partial_logit = jnp.sum(hidden * pref_out, axis=-1)
    logit = lax.psum(partial_logit, "tensor")
    prob = jax.nn.sigmoid(logit)
    numbers = jnp.arange(groups, dtype=jnp.int32)
    first = (pairs[:, :, 0][:, :, None] == numbers).astype(jnp.float32)
    second = (pairs[:, :, 1][:, :, None] == numbers).astype(jnp.float32)
    wins = jnp.sum(prob[:, :, None] * first + (1.0 - prob)[:, :, None] * second, axis=1)
    count = jnp.sum(first + second, axis=1)
    winrate = (wins + 1.0) / (count + 2.0)
    placed = (owner[:, :, None] == numbers).astype(jnp.float32)
    rowrate = jnp.sum(winrate[:, :, None] * placed, axis=1).reshape(-1)
    coef = 2.0 * (logratio - eta_scale * (rowrate - 0.5))
    weighted = (
        (
            features.astype(jnp.float32).reshape(resp_dev, -1, features.shape[1])
            * coef[:, None, None]
        )
        .reshape(features.shape)
        .astype(jnp.bfloat16)
    )
    piece = lax.all_gather(w_out, "dp", axis=0, tiled=True)
    block = weighted
    d_attn = jnp.dot(block, piece, preferred_element_type=jnp.float32).astype(jnp.bfloat16)
    total_resp = resp_dev * lax.axis_size("dp")
    block = weighted
    o_grad = (
        lax.psum_scatter(
            lax.dot_general(
                block, attn_out, (((0,), (0,)), ((), ())), preferred_element_type=jnp.float32
            ),
            "dp",
            scatter_dimension=0,
            tiled=True,
        )
        / total_resp
    )
    return (d_attn, o_grad)


def solution(mesh):
    return jax.shard_map(
        shards,
        mesh=mesh,
        in_specs=(
            P("dp", None),
            P("dp", None),
            P("dp", None, None),
            P(None, "dp", "tensor"),
            P("tensor"),
            P("tensor"),
            P("dp"),
            P("dp", "tensor"),
            P("dp", "tensor"),
            P("dp", "tensor"),
        ),
        out_specs=(P("dp", "tensor"), P("dp", "tensor")),
        check_vma=False,
    )
```

profile of v0, /device:TPU:32, one launch (start us, length us, event | category | flops | bytes accessed | tf_op | source)
XLA Modules:
  0.0 641.9 jit_solution(11647005601567376183)
XLA Ops:
  7.2 0.7 all-gather.6.cloned.1.call-update
  8.0 0.7 all-gather.4.cloned.1.call-update
  8.7 0.7 all-gather.8.cloned.1.call-update
  9.5 0.8 fusion.20
  10.3 2.2 gather_fusion.2
  12.5 0.1 reshape.146
  12.6 0.1 reshape.148
  12.7 2.2 gather_fusion.3
  14.9 0.1 reshape.151
  15.0 0.1 reshape.102
  15.2 1.2 gather_fusion.1
  16.5 1.2 gather_fusion
  17.7 168.8 %all-gather.6.cloned.1.call-done = bf16[2,4608,576]{2,1,0:T(8,128)(2,1)} async-done(((bf16[2,144,576]{2,1,0:T(8,128)(2,1)}), bf16[2,4608,576]{2,1,0:T(8,128)(2,1)}) %all-gather.6.cloned.1.call-update) | async-done | bytes 10616848 | tf_op jit(solution)/shard_map/all_gather | solution.py:23
  186.5 3.8 fusion.2
  190.3 3.9 fusion.15
  194.3 15.1 %psum.7 = f32[2,56]{1,0:T(2,128)S(1)} all-reduce(f32[2,56]{1,0:T(2,128)S(1)} %reduce_sum.39), channel_id=1, replica_groups=mesh['dp'=32,'tensor'=8] {'tensor'}, use_global_device_ids=true, to_apply=%region_1.0 | all-reduce | flops 112 | bytes 896 | tf_op jit(solution)/shard_map/psum | solution.py:29
  209.4 0.1 add_reduce_fusion.1
  209.5 0.1 select_reduce_fusion
  209.8 75.3 %all-gather.4.cloned.1.call-done = bf16[1024,4608]{0,1:T(8,128)(2,1)} async-done(((bf16[1024,576]{0,1:T(8,128)(2,1)}), bf16[1024,4608]{0,1:T(8,128)(2,1)}) %all-gather.4.cloned.1.call-update) | async-done | bytes 9437200 | tf_op jit(solution)/shard_map/all_gather | solution.py:17
  285.1 11.2 %fusion = f32[4608,512]{1,0:T(8,128)} fusion(bf16[1024,512]{1,0:T(8,128)(2,1)S(1)} %copy-done, bf16[1024,4608]{0,1:T(8,128)(2,1)} %all-gather.4.cloned.1.call-done, f32[1024]{0:T(1024)S(1)} %mul.109), kind=kOutput, calls=%fused_computation.5 | convolution fusion | flops 4845993984 | bytes 19927040 | tf_op jit(solution)/shard_map/dot_general | solution.py:55
  296.4 148.1 %all-gather.8.cloned.1.call-done = bf16[4608,512]{1,0:T(8,128)(2,1)} async-done(((bf16[144,512]{1,0:T(8,128)(2,1)}), bf16[4608,512]{1,0:T(8,128)(2,1)}) %all-gather.8.cloned.1.call-update) | async-done | bytes 4718608 | tf_op jit(solution)/shard_map/all_gather | solution.py:48
  444.5 9.8 %fusion.4 = bf16[1024,512]{1,0:T(8,128)(2,1)} fusion(bf16[4608,512]{1,0:T(8,128)(2,1)} %all-gather.8.cloned.1.call-done, bf16[1024,4608]{0,1:T(8,128)(2,1)} %all-gather.4.cloned.1.call-done, f32[1024]{0:T(1024)S(1)} %mul.109), kind=kOutput, calls=%fused_computation.11 | convolution fusion | flops 4846518272 | bytes 15208448 | tf_op jit(solution)/shard_map/dot_general | solution.py:50
  454.3 179.3 %reduce-scatter.2.cloned.1.call-done = f32[144,512]{1,0:T(8,128)} async-done(((f32[4608,512]{1,0:T(8,128)}), f32[144,512]{1,0:T(8,128)}) %reduce-scatter.2.cloned.1.call-update) | async-done | bytes 294928 | tf_op jit(solution)/shard_map/reduce_scatter | solution.py:54
  633.6 1.7 broadcast_multiply_fusion
  (35 shorter events, 0.8 us)
Async XLA Ops:
  7.2 278.0 %copy-start = (bf16[1024,512]{1,0:T(8,128)(2,1)S(1)}, bf16[1024,512]{1,0:T(8,128)(2,1)}, u32[]{:S(2)}) copy-start(bf16[1024,512]{1,0:T(8,128)(2,1)} %param.19) | copy-start | bytes 3145732
  7.2 8.0 %copy-start.2 = (bf16[16,4608]{1,0:T(8,128)(2,1)S(1)}, bf16[16,4608]{1,0:T(8,128)(2,1)}, u32[]{:S(2)}) copy-start(bf16[16,4608]{1,0:T(8,128)(2,1)} %param.12) | copy-start | bytes 442372
  7.2 179.3 %all-gather.6.cloned.1.call-start = ((), (), s32[]{:S(2)}) async-start(), calls=%async_computation.2 | async-start | bytes 12165120 | tf_op jit(solution)/shard_map/all_gather | solution.py:23
  7.9 277.2 %all-gather.4.cloned.1.call-start = ((), (), s32[]{:S(2)}) async-start(), calls=%async_computation.1 | async-start | bytes 10616832 | tf_op jit(solution)/shard_map/all_gather | solution.py:17
  8.7 435.8 %all-gather.8.cloned.1.call-start = ((), (), s32[]{:S(2)}) async-start(), calls=%async_computation.3 | async-start | bytes 4866048 | tf_op jit(solution)/shard_map/all_gather | solution.py:48
  9.4 624.2 %reduce-scatter.2.cloned.1.call-start = ((), (), s32[]{:S(2)}) async-start(), calls=%async_computation.4 | async-start | bytes 9732096 | tf_op jit(solution)/shard_map/reduce_scatter | solution.py:54
  16.4 173.9 %copy-start.3 = (f32[576]{0:T(1024)S(1)}, f32[576]{0:T(1024)}, u32[]{:S(2)}) copy-start(f32[576]{0:T(1024)} %param.17) | copy-start | bytes 6916
  16.4 173.9 %copy-start.4 = (f32[576]{0:T(1024)S(1)}, f32[576]{0:T(1024)}, u32[]{:S(2)}) copy-start(f32[576]{0:T(1024)} %param.16) | copy-start | bytes 6916
  17.6 191.9 %copy-start.1 = (s32[2,8]{1,0:T(2,128)S(1)}, s32[2,8]{1,0:T(2,128)}, u32[]{:S(2)}) copy-start(s32[2,8]{1,0:T(2,128)} %param.13) | copy-start | bytes 196
  17.6 192.0 %copy-start.5 = (f32[16]{0:T(128)S(1)}, f32[16]{0:T(128)}, u32[]{:S(2)}) copy-start(f32[16]{0:T(128)} %param.18) | copy-start | bytes 196
Sparse Core Ops, SparseCore 0:
  9.8 176.6 all-gather.5
  188.3 96.7 all-gather.3
  286.9 157.4 all-gather.7
  446.9 186.7 reduce-scatter.1
where the time goes:
time: 642 us
  waiting for transfers between devices  574 us (89%)
  matrix products  28.8 us (4%)
  blocking collectives  15.1 us (2%)
  between operations  13.9 us (2%)
  local copies, waits for them, and re-layouts  8.34 us (1%)
    reduce_scatter x1, waiting for transfers between devices, shards(): lax.psum_scatter(lax.dot_general(block, attn_out, (((0,), (0,)), ((), ())...  179 us
    all_gather x1, waiting for transfers between devices, shards(): piece = lax.all_gather(pref_weight, 'dp', axis=1, tiled=True)  169 us
    all_gather x1, waiting for transfers between devices, shards(): piece = lax.all_gather(w_out, 'dp', axis=0, tiled=True)  148 us
    all_gather x1, waiting for transfers between devices, shards(): features = lax.all_gather(grad_out, 'tensor', axis=1, tiled=True)  75.3 us
    psum x1, blocking collectives, shards(): logit = lax.psum(partial_logit, 'tensor')  15.1 us
  transfers between devices with their start and end apart: 4, of which 4 were waited for; matrix products, arithmetic and copies ran while one was open for 6% of the time, Pallas kernels for 0%

commit v1 on v0

--- a/solution.py
+++ b/solution.py
@@ -4,6 +4,11 @@
 from jax.sharding import PartitionSpec as P
 
 eta_scale = 2.0
+
+
+def exchange_gather(x, name, dim):
+    repeated = jnp.stack([x] * lax.axis_size(name))
+    return jnp.concatenate(lax.all_to_all(repeated, name, 0, 0), axis=dim)
 
 
 def shards(
@@ -14,7 +19,7 @@
     groups = owner.shape[1]
     npairs = pairs.shape[1]
     width_local = pref_weight.shape[2]
-    features = lax.all_gather(grad_out, "tensor", axis=1, tiled=True)
+    features = exchange_gather(grad_out, "tensor", 1)
     base = (jnp.arange(prompts_dev, dtype=jnp.int32) * groups)[:, None]
     row_a = base + jnp.take_along_axis(owner, pairs[:, :, 0], axis=1)
     row_b = base + jnp.take_along_axis(owner, pairs[:, :, 1], axis=1)

time: 642 us -> 719 us (1.12)
  waiting for transfers between devices: 574 us -> 627 us
  other arithmetic: 2.02 us -> 12.2 us
  starting transfers between devices: 0.15 us -> 7.81 us
    all_gather x1, waiting for transfers between devices: 169 us -> 330 us  [shards(): piece = lax.all_gather(pref_weight, 'dp', axis=1, tiled=True)]
    all_gather x1 -> x0, waiting for transfers between devices: 75.3 us -> none  [shards(): features = lax.all_gather(grad_out, 'tensor', axis=1, tiled=True)]
    all_gather x1, waiting for transfers between devices: 148 us -> 115 us  [shards(): piece = lax.all_gather(w_out, 'dp', axis=0, tiled=True)]
    convert_element_type x0 -> x1, other arithmetic: none -> 10.2 us  [shards(): weighted = (features.astype(jnp.float32).reshape(resp_dev, -1, features.s...]
    all_to_all x0 -> x1, starting transfers between devices: none -> 7.7 us  [exchange_gather(): return jnp.concatenate(lax.all_to_all(repeated, name, 0, 0), axis=dim)]
  transfers between devices with their start and end apart: 4 -> 4, of which waited for: 4 -> 3; matrix products, arithmetic and copies ran while one was open for 6% -> 7% of each run, Pallas kernels for 0% -> 0%
where the time goes in v1:
time: 719 us; the launch traced here: 718 us
  waiting for transfers between devices  627 us (87%)
  matrix products  28.8 us (4%)
  blocking collectives  15.4 us (2%)
  between operations  13.9 us (2%)
  local copies, waits for them, and re-layouts  13.4 us (2%)
  other arithmetic  12.2 us (2%)
  starting transfers between devices  7.81 us (1%)
    all_gather x1, waiting for transfers between devices, shards(): piece = lax.all_gather(pref_weight, 'dp', axis=1, tiled=True)  330 us
    reduce_scatter x1, waiting for transfers between devices, shards(): lax.psum_scatter(lax.dot_general(block, attn_out, (((0,), (0,)), ((), ())...  180 us
    all_gather x1, waiting for transfers between devices, shards(): piece = lax.all_gather(w_out, 'dp', axis=0, tiled=True)  115 us
    psum x1, blocking collectives, shards(): logit = lax.psum(partial_logit, 'tensor')  15.4 us
  transfers between devices with their start and end apart: 4, of which 3 were waited for; matrix products, arithmetic and copies ran while one was open for 7% of the time, Pallas kernels for 0%

profile of v1, /device:TPU:32, one launch (start us, length us, event | category | flops | bytes accessed | tf_op | source)
XLA Modules:
  0.0 718.3 jit_solution(8513090795073435907)
XLA Ops:
  7.2 0.7 all-gather.3.cloned.1.call-update
  7.9 6.2 stack.2
  14.1 7.7 %all-to-all-start = ((bf16[8,1024,576]{1,2,0:T(8,128)(2,1)}), bf16[8,1024,576]{1,2,0:T(8,128)(2,1)}, u32[]{:S(2)}, u32[]{:S(2)}) async-start(bf16[8,1024,576]{1,2,0:T(8,128)(2,1)} %stack.2), calls=%async_computation | async-start | bytes 18874368 | tf_op jit(solution)/shard_map/all_to_all | solution.py:11
  21.8 0.7 all-gather.5.cloned.1.call-update
  22.6 0.1 reshape.152
  22.7 2.0 gather_fusion.2
  24.7 0.1 reshape.155
  24.8 0.1 reshape.157
  24.9 2.0 gather_fusion.3
  27.1 0.1 reshape.110
  27.3 1.2 gather_fusion.1
  28.5 1.2 gather_fusion
  29.7 330.4 %all-gather.3.cloned.1.call-done = bf16[2,4608,576]{2,1,0:T(8,128)(2,1)} async-done(((bf16[2,144,576]{2,1,0:T(8,128)(2,1)}), bf16[2,4608,576]{2,1,0:T(8,128)(2,1)}) %all-gather.3.cloned.1.call-update) | async-done | bytes 10616848 | tf_op jit(solution)/shard_map/all_gather | solution.py:28
  360.1 3.8 fusion.1
  363.9 4.0 fusion.13
  368.0 15.4 %psum.7 = f32[2,56]{1,0:T(2,128)S(1)} all-reduce(f32[2,56]{1,0:T(2,128)S(1)} %reduce_sum.39), channel_id=1, replica_groups=mesh['dp'=32,'tensor'=8] {'tensor'}, use_global_device_ids=true, to_apply=%region_1.0 | all-reduce | flops 112 | bytes 896 | tf_op jit(solution)/shard_map/psum | solution.py:34
  383.4 0.1 add_reduce_fusion.1
  383.5 0.1 select_reduce_fusion
  383.9 10.2 %fusion = bf16[1024,4608]{0,1:T(8,128)(2,1)} fusion(f32[1024]{0:T(1024)S(1)} %mul.109, bf16[8,1024,576]{1,2,0:T(8,128)(2,1)} %all-to-all-done), kind=kLoop, calls=%fused_computation.5 | loop fusion | flops 14155776 | bytes 18878464 | tf_op jit(solution)/shard_map/convert_element_type | solution.py:51
  394.1 11.2 %fusion.19 = f32[4608,512]{1,0:T(8,128)} fusion(bf16[1024,4608]{0,1:T(8,128)(2,1)} %fusion, bf16[1024,512]{1,0:T(8,128)(2,1)S(1)} %copy-done), kind=kOutput, calls=%fused_computation.52 | convolution fusion | flops 4831838208 | bytes 19922944 | tf_op jit(solution)/shard_map/dot_general | solution.py:60
  405.3 115.1 %all-gather.5.cloned.1.call-done = bf16[4608,512]{1,0:T(8,128)(2,1)} async-done(((bf16[144,512]{1,0:T(8,128)(2,1)}), bf16[4608,512]{1,0:T(8,128)(2,1)}) %all-gather.5.cloned.1.call-update) | async-done | bytes 4718608 | tf_op jit(solution)/shard_map/all_gather | solution.py:53
  520.4 9.8 %convolution_convert_fusion = bf16[1024,512]{1,0:T(8,128)(2,1)} fusion(bf16[1024,4608]{0,1:T(8,128)(2,1)} %fusion, bf16[4608,512]{1,0:T(8,128)(2,1)} %all-gather.5.cloned.1.call-done), kind=kOutput, calls=%fused_computation.10 | convolution fusion | flops 4832362496 | bytes 15204352 | tf_op jit(solution)/shard_map/dot_general | solution.py:55
  530.2 179.9 %reduce-scatter.2.cloned.1.call-done = f32[144,512]{1,0:T(8,128)} async-done(((f32[4608,512]{1,0:T(8,128)}), f32[144,512]{1,0:T(8,128)}) %reduce-scatter.2.cloned.1.call-update) | async-done | bytes 294928 | tf_op jit(solution)/shard_map/reduce_scatter | solution.py:59
  710.1 1.7 broadcast_multiply_fusion
  (38 shorter events, 0.8 us)
Async XLA Ops:
  7.2 386.9 %copy-start = (bf16[1024,512]{1,0:T(8,128)(2,1)S(1)}, bf16[1024,512]{1,0:T(8,128)(2,1)}, u32[]{:S(2)}) copy-start(bf16[1024,512]{1,0:T(8,128)(2,1)} %param.19) | copy-start | bytes 3145732
  7.2 352.9 %all-gather.3.cloned.1.call-start = ((), (), s32[]{:S(2)}) async-start(), calls=%async_computation.2 | async-start | bytes 12165120 | tf_op jit(solution)/shard_map/all_gather | solution.py:28
  14.1 8.5 %copy-start.3 = (s32[2,56,2]{1,2,0:T(2,128)S(1)}, s32[2,56,2]{1,2,0:T(2,128)}, u32[]{:S(2)}) copy-start(s32[2,56,2]{1,2,0:T(2,128)} %param.14) | copy-start | bytes 2692
  14.1 8.6 %copy-start.1 = (s32[2,8]{1,0:T(2,128)S(1)}, s32[2,8]{1,0:T(2,128)}, u32[]{:S(2)}) copy-start(s32[2,8]{1,0:T(2,128)} %param.13) | copy-start | bytes 196
  14.1 13.2 %copy-start.2 = (bf16[16,4608]{1,0:T(8,128)(2,1)S(1)}, bf16[16,4608]{1,0:T(8,128)(2,1)}, u32[]{:S(2)}) copy-start(bf16[16,4608]{1,0:T(8,128)(2,1)} %param.12) | copy-start | bytes 442372
  14.1 369.8 %all-to-all-start = ((bf16[8,1024,576]{1,2,0:T(8,128)(2,1)}), bf16[8,1024,576]{1,2,0:T(8,128)(2,1)}, u32[]{:S(2)}, u32[]{:S(2)}) async-start(bf16[8,1024,576]{1,2,0:T(8,128)(2,1)} %stack.2), calls=%async_computation | async-start | bytes 18874368 | tf_op jit(solution)/shard_map/all_to_all | solution.py:11
  21.8 498.6 %all-gather.5.cloned.1.call-start = ((), (), s32[]{:S(2)}) async-start(), calls=%async_computation.3 | async-start | bytes 4866048 | tf_op jit(solution)/shard_map/all_gather | solution.py:53
  22.5 687.6 %reduce-scatter.2.cloned.1.call-start = ((), (), s32[]{:S(2)}) async-start(), calls=%async_computation.4 | async-start | bytes 9732096 | tf_op jit(solution)/shard_map/reduce_scatter | solution.py:59
  28.4 335.5 %copy-start.4 = (f32[576]{0:T(1024)S(1)}, f32[576]{0:T(1024)}, u32[]{:S(2)}) copy-start(f32[576]{0:T(1024)} %param.17) | copy-start | bytes 6916
  28.5 335.5 %copy-start.5 = (f32[576]{0:T(1024)S(1)}, f32[576]{0:T(1024)}, u32[]{:S(2)}) copy-start(f32[576]{0:T(1024)} %param.16) | copy-start | bytes 6916
  29.7 354.1 %copy-start.6 = (f32[16]{0:T(128)S(1)}, f32[16]{0:T(128)}, u32[]{:S(2)}) copy-start(f32[16]{0:T(128)} %param.18) | copy-start | bytes 196
Sparse Core Ops, SparseCore 0:
  9.8 350.2 all-gather.2
  361.8 158.5 all-gather.4
  523.0 187.0 reduce-scatter.1
